TPU v7x, 512 devices: a whole 4x8x8 slice. The times are simulated.
512 devices in a mesh: pairs: 64 (over x, y, core), aux: 8 (over z).
Axes of the slice: x: 4, y: 8, z: 8, core: 2. Of those that a mesh axis runs over, the one named last changes fastest.
Arguments:
- amplitudes: bfloat16 [1024, 128, 128], P('pairs'), may hold values from -6 to 6
- pno_coef: bfloat16 [1024, 256, 128], P('pairs'), may hold values from -0.625 to 0.625
- ladder_ints: bfloat16 [320, 128, 128], P('aux'), may hold values from -0.3125 to 0.3125
- coulomb_ints: bfloat16 [1024, 128, 128], P(('pairs', 'aux')), may hold values from -6 to 6
- pno_energy: float32 [1024, 128], P(('pairs', 'aux')), may hold values from 0.3 to 3
- link_owner: int32 [49152, 1], P(('pairs', 'aux')), may hold values from 0 to 63; in each aligned block of 96 rows (0 to 95, 96 to 191, ...) at most 2 rows name the same one
- link_local: int32 [49152, 1], P(('pairs', 'aux')), may hold values from 0 to 15
Outputs:
- updated: float32 [1024, 128, 128], P(('pairs', 'aux'))
Inputs may be any that keep to these rules, and one draw needn't show every extreme that they name: `link_owner`: in each device's aligned block of 96 rows no owner group is named by more than 2 rows, a bound that some block reaches.
All inputs are finite; a program needn't handle non-finite values.
Results may differ from a plain program's by a relative error of at most 0.0033.
Values may be sent and summed in bfloat16 or wider, within the bound.
No kernel may reach another device: no remote copies, remote signals or barrier semaphores. Data moves between devices by JAX's collectives and lax.ppermute only.
A program may use at most 128 MiB of HBM per device.

v0:
```python
import jax
import jax.numpy as jnp
from jax import lax
from jax.sharding import PartitionSpec as P


def local(amplitudes, pno_coef, ladder_ints, coulomb_ints, pno_energy, link_owner, link_local):
    groups = lax.axis_size("pairs")
    pair_dev = amplitudes.shape[0]
    own_rows = coulomb_ints.shape[0]
    slot_count = link_owner.shape[0]
    per_slice = slot_count // pair_dev
    capacity = max(2, (5 * slot_count + 4 * groups - 1) // (4 * groups))
    pno_width = amplitudes.shape[1]
    pao_width = pno_coef.shape[1]
    owner_group = link_owner[:, 0]
    local_index = link_local[:, 0]
    slot_order = jnp.arange(slot_count, dtype=jnp.int32)
    same_owner = (owner_group[:, None] == owner_group[None, :]) & (
        slot_order[None, :] < slot_order[:, None]
    )
    slot_rank = jnp.sum(same_owner.astype(jnp.int32), axis=1)
    bucket = owner_group * capacity + slot_rank
    places = jnp.arange(groups * capacity, dtype=jnp.int32)
    match_table = (bucket[:, None] == places[None, :]).astype(jnp.int32)
    wanted = jnp.sum(match_table * (local_index[:, None] + 1), axis=0) - 1
    asked_rows = lax.all_to_all(
        wanted.reshape(groups, capacity), "pairs", split_axis=0, concat_axis=0, tiled=True
    )
    present = asked_rows >= 0
    picked = jnp.maximum(asked_rows, 0)
    nothing = jnp.zeros((), jnp.bfloat16)
    amp_items = jnp.where(present[:, :, None, None], amplitudes[picked], nothing)
    coef_items = jnp.where(present[:, :, None, None], pno_coef[picked], nothing)
    got_amp, got_coef = (
        lax.all_to_all(amp_items, "pairs", split_axis=0, concat_axis=0, tiled=True),
        lax.all_to_all(coef_items, "pairs", split_axis=0, concat_axis=0, tiled=True),
    )
    flat_amp = got_amp.reshape(groups * capacity, pno_width, pno_width)
    flat_coef = got_coef.reshape(groups * capacity, pao_width, pno_width)
    key_rows = bucket.reshape(pair_dev, per_slice)

    def pair_terms(inputs):
        coef_p, amp_p, key_row = inputs
        coef_q = flat_coef[key_row]
        amp_q = flat_amp[key_row]
        intersection = jnp.einsum(
            "ac,lad->lcd", coef_p, coef_q, preferred_element_type=jnp.float32
        ).astype(jnp.bfloat16)
        halfway = jnp.einsum(
            "lcd,lde->lce", intersection, amp_q, preferred_element_type=jnp.float32
        ).astype(jnp.bfloat16)
        total = jnp.einsum("lce,lfe->cf", halfway, intersection, preferred_element_type=jnp.float32)
        ladder_half = jnp.einsum(
            "qcd,de->qce", ladder_ints, amp_p, preferred_element_type=jnp.float32
        ).astype(jnp.bfloat16)
        total = total + jnp.einsum(
            "qce,qfe->cf", ladder_half, ladder_ints, preferred_element_type=jnp.float32
        )
        return total

    partial_value = lax.map(pair_terms, (pno_coef, amplitudes, key_rows))
    first_row = lax.axis_index("aux") * own_rows
    amp_mine = lax.dynamic_slice_in_dim(amplitudes, first_row, own_rows, 0)
    summed = lax.psum(partial_value, "aux")
    reduced = lax.dynamic_slice_in_dim(summed, first_row, own_rows, 0)
    residual = coulomb_ints.astype(jnp.float32) + reduced
    denominator = pno_energy[:, :, None] + pno_energy[:, None, :]
    return amp_mine.astype(jnp.float32) - residual / denominator


def solution(mesh):
    in_specs = (
        P("pairs", None, None),
        P("pairs", None, None),
        P("aux", None, None),
        P(("pairs", "aux"), None, None),
        P(("pairs", "aux"), None),
        P(("pairs", "aux"), None),
        P(("pairs", "aux"), None),
    )
    out_specs = P(("pairs", "aux"), None, None)
    return jax.shard_map(local, mesh=mesh, in_specs=in_specs, out_specs=out_specs, check_vma=False)
```

profile of v0, /device:TPU:2, one launch (start us, length us, event | category | flops | bytes accessed | tf_op | source)
XLA Modules:
  0.0 579.0 jit_solution(16118599690050762865)
XLA Ops:
  6.5 0.9 convert_reduce_fusion
  7.4 0.7 fusion.21
  8.1 0.7 add_bitcast_fusion
  9.0 19.1 %all_to_all.16 = s32[64,1,2]{2,1,0:T(1,128)S(1)} all-to-all(s32[64,1,2]{2,1,0:T(1,128)S(1)} %bitcast.97), channel_id=1, replica_groups=mesh['pairs'=64,'aux'=8] {'pairs'}, dimensions={0} | all-to-all | bytes 1024 | tf_op jit(solution)/shard_map/all_to_all | solution.py:27
  28.6 4.1 gather_fusion.3
  32.7 4.5 broadcast_select_fusion.1
  37.2 6.6 %all-to-all-start.2 = ((bf16[64,2,128,128]{3,2,1,0:T(8,128)(2,1)}), bf16[64,2,128,128]{3,2,1,0:T(8,128)(2,1)}, u32[]{:S(2)}, u32[]{:S(2)}) async-start(bf16[64,2,128,128]{3,2,1,0:T(8,128)(2,1)} %broadcast_select_fusion.1), calls=%async_computation.2 | async-start | bytes 8388608 | tf_op jit(solution)/shard_map/all_to_all | solution.py:36
  43.8 6.6 %gather_fusion.2 = bf16[128,256,128]{2,1,0:T(8,128)(2,1)} fusion(bf16[16,256,128]{2,1,0:T(8,128)(2,1)S(1)} %copy-done.1, s32[1024]{0:T(1024)S(1)} %pad_clamp_fusion.1), kind=kCustom, calls=%fused_computation.2 | custom fusion | bytes 16777728 | tf_op jit(solution)/shard_map/gather | solution.py:34
  50.4 7.2 %broadcast_select_fusion = bf16[64,2,256,128]{3,2,1,0:T(8,128)(2,1)} fusion(bf16[64,2,256,128]{3,2,1,0:T(8,128)(2,1)} %bitcast.95, pred[64,2]{1,0:T(8,128)(4,1)S(1)} %copy.33), kind=kLoop, calls=%fused_computation.27 | loop fusion | flops 4194304 | bytes 16777344 | tf_op jit(solution)/shard_map/jit(_where)/select_n | solution.py:34
  57.6 81.1 %all-to-all-done.2 = bf16[64,2,128,128]{3,2,1,0:T(8,128)(2,1)} async-done(((bf16[64,2,128,128]{3,2,1,0:T(8,128)(2,1)}), bf16[64,2,128,128]{3,2,1,0:T(8,128)(2,1)}, u32[]{:S(2)}, u32[]{:S(2)}) %all-to-all-start.2) | async-done | bytes 4194336 | tf_op jit(solution)/shard_map/all_to_all | solution.py:36
  138.7 7.0 %all-to-all-start.1 = ((bf16[64,2,256,128]{3,2,1,0:T(8,128)(2,1)}), bf16[64,2,256,128]{3,2,1,0:T(8,128)(2,1)}, u32[]{:S(2)}, u32[]{:S(2)}) async-start(bf16[64,2,256,128]{3,2,1,0:T(8,128)(2,1)} %broadcast_select_fusion), calls=%async_computation.1 | async-start | bytes 16777216 | tf_op jit(solution)/shard_map/all_to_all | solution.py:37
  145.9 184.1 %all-to-all-done.1 = bf16[64,2,256,128]{3,2,1,0:T(8,128)(2,1)} async-done(((bf16[64,2,256,128]{3,2,1,0:T(8,128)(2,1)}), bf16[64,2,256,128]{3,2,1,0:T(8,128)(2,1)}, u32[]{:S(2)}, u32[]{:S(2)}) %all-to-all-start.1) | async-done | bytes 8388640 | tf_op jit(solution)/shard_map/all_to_all | solution.py:37
  330.0 156.9 %while.10 = (s32[]{:T(128)}, f32[16,128,128]{2,1,0:T(8,128)}, s32[16,6]{1,0:T(8,128)S(1)}, bf16[128,256,128]{2,1,0:T(8,128)(2,1)}, bf16[16,256,128]{2,1,0:T(8,12...) while((s32[]{:T(128)}, f32[16,128,128]{2,1,0:T(8,128)}, ...), condition=%wide.region_3.4_spmd, body=%wide.region_2.3_spmd.sunk | while | flops 437076992 | bytes 5084381 | solution.py:62
  330.0 4.0 gather_fusion
  334.4 2.8 gather_fusion.1
  337.6 2.3 fusion.48
  339.9 4.0 gather_fusion
  344.2 2.8 gather_fusion.1
  347.4 2.3 fusion.48
  349.7 4.0 gather_fusion
  354.0 2.8 gather_fusion.1
  357.2 2.3 fusion.48
  359.5 4.0 gather_fusion
  363.8 2.8 gather_fusion.1
  367.0 2.3 fusion.48
  369.3 4.0 gather_fusion
  373.6 2.8 gather_fusion.1
  376.4 0.4 fusion.47
  376.8 2.3 fusion.48
  379.1 4.0 gather_fusion
  383.4 2.8 gather_fusion.1
  386.6 2.3 fusion.48
  388.9 4.0 gather_fusion
  393.2 2.8 gather_fusion.1
  396.4 2.3 fusion.48
  398.7 4.0 gather_fusion
  403.0 2.8 gather_fusion.1
  406.2 2.3 fusion.48
  408.5 4.0 gather_fusion
  412.8 2.8 gather_fusion.1
  416.0 2.3 fusion.48
  418.3 4.0 gather_fusion
  422.6 2.8 gather_fusion.1
  425.8 2.3 fusion.48
  428.1 4.0 gather_fusion
  432.4 2.8 gather_fusion.1
  435.6 2.3 fusion.48
  437.9 4.0 gather_fusion
  442.2 2.8 gather_fusion.1
  445.4 2.3 fusion.48
  447.7 4.0 gather_fusion
  452.0 2.8 gather_fusion.1
  455.2 2.3 fusion.48
  457.5 4.0 gather_fusion
  461.8 2.8 gather_fusion.1
  465.0 2.3 fusion.48
  467.3 4.0 gather_fusion
  471.6 2.8 gather_fusion.1
  474.8 2.3 fusion.48
  477.1 4.0 gather_fusion
  481.4 2.8 gather_fusion.1
  484.6 2.3 fusion.48
  486.9 83.6 %all-reduce.2.cloned.1.call-done = f32[16,128,128]{2,1,0:T(8,128)} async-done(((f32[16,128,128]{2,1,0:T(8,128)}), f32[16,128,128]{2,1,0:T(8,128)}) %all-reduce.2.cloned.1.call-update) | async-done | bytes 1048592 | tf_op jit(solution)/shard_map/psum | solution.py:65
  570.5 1.7 divide_subtract_fusion
  (86 shorter events, 12.3 us)
Async XLA Ops:
  37.2 6.6 %copy-start.1 = (bf16[16,256,128]{2,1,0:T(8,128)(2,1)S(1)}, bf16[16,256,128]{2,1,0:T(8,128)(2,1)}, u32[]{:S(2)}) copy-start(bf16[16,256,128]{2,1,0:T(8,128)(2,1)} %param.10) | copy-start | bytes 3145732
  37.2 101.5 %all-to-all-start.2 = ((bf16[64,2,128,128]{3,2,1,0:T(8,128)(2,1)}), bf16[64,2,128,128]{3,2,1,0:T(8,128)(2,1)}, u32[]{:S(2)}, u32[]{:S(2)}) async-start(bf16[64,2,128,128]{3,2,1,0:T(8,128)(2,1)} %broadcast_select_fusion.1), calls=%async_computation.2 | async-start | bytes 8388608 | tf_op jit(solution)/shard_map/all_to_all | solution.py:36
  57.6 272.4 %copy-start = (bf16[40,128,128]{2,1,0:T(8,128)(2,1)S(1)}, bf16[40,128,128]{2,1,0:T(8,128)(2,1)}, u32[]{:S(2)}) copy-start(bf16[40,128,128]{2,1,0:T(8,128)(2,1)} %param.11) | copy-start | bytes 3932164
  138.7 191.3 %all-to-all-start.1 = ((bf16[64,2,256,128]{3,2,1,0:T(8,128)(2,1)}), bf16[64,2,256,128]{3,2,1,0:T(8,128)(2,1)}, u32[]{:S(2)}, u32[]{:S(2)}) async-start(bf16[64,2,256,128]{3,2,1,0:T(8,128)(2,1)} %broadcast_select_fusion), calls=%async_computation.1 | async-start | bytes 16777216 | tf_op jit(solution)/shard_map/all_to_all | solution.py:37
  145.6 424.8 %all-reduce.2.cloned.1.call-start = ((), (), s32[]{:S(2)}) async-start(), calls=%async_computation.3 | async-start | bytes 2097152 | tf_op jit(solution)/shard_map/psum | solution.py:65
  330.0 240.5 %copy-start.2 = (bf16[2,128,128]{2,1,0:T(8,128)(2,1)S(1)}, bf16[2,128,128]{2,1,0:T(8,128)(2,1)}, u32[]{:S(2)}) copy-start(bf16[2,128,128]{2,1,0:T(8,128)(2,1)} %param.12) | copy-start | bytes 196612
  330.0 240.5 %copy-start.3 = (f32[2,128]{1,0:T(2,128)S(1)}, f32[2,128]{1,0:T(2,128)}, u32[]{:S(2)}) copy-start(f32[2,128]{1,0:T(2,128)} %param.13) | copy-start | bytes 3076
Sparse Core Ops, SparseCore 0:
  487.0 83.4 all-reduce.1
where the time goes:
time: 582 us; the launch traced here: 579 us
  waiting for transfers between devices  349 us (60%)
  local copies, waits for them, and re-layouts  120 us (21%)
  matrix products  47.7 us (8%)
  blocking collectives  19.1 us (3%)
  other arithmetic  16.2 us (3%)
  starting transfers between devices  13.6 us (2%)
  between operations  13.5 us (2%)
    all_to_all x1, waiting for transfers between devices, local(): lax.all_to_all(coef_items, 'pairs', split_axis=0, concat_axis=0, tiled=True)  184 us
    psum x1, waiting for transfers between devices, local(): summed = lax.psum(partial_value, 'aux')  83.6 us
    all_to_all x1, waiting for transfers between devices, local(): lax.all_to_all(amp_items, 'pairs', split_axis=0, concat_axis=0, tiled=True)  81.1 us
    gather x16, local copies, waits for them, and re-layouts, pair_terms(): coef_q = flat_coef[key_row]  64 us
    gather x16, local copies, waits for them, and re-layouts, pair_terms(): amp_q = flat_amp[key_row]  44.3 us
    dot_general x16, matrix products, pair_terms(): jnp.einsum('qce,qfe->cf', ladder_half, ladder_ints, preferred_element_typ...  36.2 us
    all_to_all x1, blocking collectives, local(): lax.all_to_all(wanted.reshape(groups, capacity), 'pairs', split_axis=0, c...  19.1 us
  transfers between devices with their start and end apart: 3, of which 3 were waited for; matrix products, arithmetic and copies ran while one was open for 2% of the time, Pallas kernels for 0%

commit v1 on v0

--- a/solution.py
+++ b/solution.py
@@ -62,7 +62,7 @@
     partial_value = lax.map(pair_terms, (pno_coef, amplitudes, key_rows))
     first_row = lax.axis_index("aux") * own_rows
     amp_mine = lax.dynamic_slice_in_dim(amplitudes, first_row, own_rows, 0)
-    summed = lax.psum(partial_value, "aux")
+    summed = jnp.sum(lax.all_gather(partial_value, "aux"), axis=0)
     reduced = lax.dynamic_slice_in_dim(summed, first_row, own_rows, 0)
     residual = coulomb_ints.astype(jnp.float32) + reduced
     denominator = pno_energy[:, :, None] + pno_energy[:, None, :]

time: 582 us -> 602 us (1.034)
  the two profiles are of different devices: /device:TPU:2 before, /device:TPU:1 now
where the time goes in v1:
time: 602 us; the launch traced here: 599 us
  waiting for transfers between devices  365 us (61%)
  local copies, waits for them, and re-layouts  120 us (20%)
  matrix products  47.7 us (8%)
  blocking collectives  20.7 us (3%)
  other arithmetic  20.3 us (3%)
  between operations  13.5 us (2%)
  starting transfers between devices  11.9 us (2%)
    all_to_all x1, waiting for transfers between devices, local(): lax.all_to_all(coef_items, 'pairs', split_axis=0, concat_axis=0, tiled=True)  186 us
    all_gather x1, waiting for transfers between devices, local(): summed = jnp.sum(lax.all_gather(partial_value, 'aux'), axis=0)  97.5 us
    all_to_all x1, waiting for transfers between devices, local(): lax.all_to_all(amp_items, 'pairs', split_axis=0, concat_axis=0, tiled=True)  82.1 us
    gather x16, local copies, waits for them, and re-layouts, pair_terms(): coef_q = flat_coef[key_row]  64 us
    gather x16, local copies, waits for them, and re-layouts, pair_terms(): amp_q = flat_amp[key_row]  44.3 us
    dot_general x16, matrix products, pair_terms(): jnp.einsum('qce,qfe->cf', ladder_half, ladder_ints, preferred_element_typ...  36.2 us
    all_to_all x1, blocking collectives, local(): lax.all_to_all(wanted.reshape(groups, capacity), 'pairs', split_axis=0, c...  20.7 us
  transfers between devices with their start and end apart: 3, of which 3 were waited for; matrix products, arithmetic and copies ran while one was open for 2% of the time, Pallas kernels for 0%

profile of v1, /device:TPU:1, one launch (start us, length us, event | category | flops | bytes accessed | tf_op | source)
XLA Modules:
  0.0 599.4 jit_solution(631277813605695512)
XLA Ops:
  6.5 0.9 convert_reduce_fusion
  7.4 0.7 fusion.21
  8.1 0.7 add_bitcast_fusion
  9.0 20.7 %all_to_all.16 = s32[64,1,2]{2,1,0:T(1,128)S(1)} all-to-all(s32[64,1,2]{2,1,0:T(1,128)S(1)} %bitcast.99), channel_id=1, replica_groups=mesh['pairs'=64,'aux'=8] {'pairs'}, dimensions={0} | all-to-all | bytes 1024 | tf_op jit(solution)/shard_map/all_to_all | solution.py:27
  30.3 4.1 gather_fusion.3
  34.3 4.5 broadcast_select_fusion.1
  38.8 5.8 all-to-all-start.2
  44.7 6.6 %gather_fusion.2 = bf16[128,256,128]{2,1,0:T(8,128)(2,1)} fusion(bf16[16,256,128]{2,1,0:T(8,128)(2,1)S(1)} %copy-done.1, s32[1024]{0:T(1024)S(1)} %pad_clamp_fusion.1), kind=kCustom, calls=%fused_computation.2 | custom fusion | bytes 16777728 | tf_op jit(solution)/shard_map/gather | solution.py:34
  51.2 7.2 %broadcast_select_fusion = bf16[64,2,256,128]{3,2,1,0:T(8,128)(2,1)} fusion(bf16[64,2,256,128]{3,2,1,0:T(8,128)(2,1)} %bitcast.96, pred[64,2]{1,0:T(8,128)(4,1)S(1)} %copy.33), kind=kLoop, calls=%fused_computation.27 | loop fusion | flops 4194304 | bytes 16777344 | tf_op jit(solution)/shard_map/jit(_where)/select_n | solution.py:34
  58.5 82.1 %all-to-all-done.2 = bf16[64,2,128,128]{3,2,1,0:T(8,128)(2,1)} async-done(((bf16[64,2,128,128]{3,2,1,0:T(8,128)(2,1)}), bf16[64,2,128,128]{3,2,1,0:T(8,128)(2,1)}, u32[]{:S(2)}, u32[]{:S(2)}) %all-to-all-start.2) | async-done | bytes 4194336 | tf_op jit(solution)/shard_map/all_to_all | solution.py:36
  140.6 6.0 %all-to-all-start.1 = ((bf16[64,2,256,128]{3,2,1,0:T(8,128)(2,1)}), bf16[64,2,256,128]{3,2,1,0:T(8,128)(2,1)}, u32[]{:S(2)}, u32[]{:S(2)}) async-start(bf16[64,2,256,128]{3,2,1,0:T(8,128)(2,1)} %broadcast_select_fusion), calls=%async_computation.1 | async-start | bytes 16777216 | tf_op jit(solution)/shard_map/all_to_all | solution.py:37
  146.8 185.5 %all-to-all-done.1 = bf16[64,2,256,128]{3,2,1,0:T(8,128)(2,1)} async-done(((bf16[64,2,256,128]{3,2,1,0:T(8,128)(2,1)}), bf16[64,2,256,128]{3,2,1,0:T(8,128)(2,1)}, u32[]{:S(2)}, u32[]{:S(2)}) %all-to-all-start.1) | async-done | bytes 8388640 | tf_op jit(solution)/shard_map/all_to_all | solution.py:37
  332.4 156.8 %while.10 = (s32[]{:T(128)}, f32[16,128,128]{2,1,0:T(8,128)}, s32[16,6]{1,0:T(8,128)S(1)}, bf16[128,256,128]{2,1,0:T(8,128)(2,1)}, bf16[16,256,128]{2,1,0:T(8,12...) while((s32[]{:T(128)}, f32[16,128,128]{2,1,0:T(8,128)}, ...), condition=%wide.region_3.4_spmd, body=%wide.region_2.3_spmd.sunk | while | flops 437076992 | bytes 5084381 | solution.py:62
  332.4 4.0 gather_fusion
  336.7 2.8 gather_fusion.1
  339.9 2.3 fusion.48
  342.2 4.0 gather_fusion
  346.6 2.8 gather_fusion.1
  349.7 2.3 fusion.48
  352.0 4.0 gather_fusion
  356.3 2.8 gather_fusion.1
  359.5 2.3 fusion.48
  361.8 4.0 gather_fusion
  366.1 2.8 gather_fusion.1
  369.3 2.3 fusion.48
  371.6 4.0 gather_fusion
  375.9 2.8 gather_fusion.1
  379.1 2.3 fusion.48
  381.4 4.0 gather_fusion
  385.7 2.8 gather_fusion.1
  388.9 2.3 fusion.48
  391.2 4.0 gather_fusion
  395.5 2.8 gather_fusion.1
  398.7 2.3 fusion.48
  401.0 4.0 gather_fusion
  405.3 2.8 gather_fusion.1
  408.5 2.3 fusion.48
  410.8 4.0 gather_fusion
  415.1 2.8 gather_fusion.1
  418.3 2.3 fusion.48
  420.6 4.0 gather_fusion
  424.9 2.8 gather_fusion.1
  428.1 2.3 fusion.48
  430.4 4.0 gather_fusion
  434.7 2.8 gather_fusion.1
  437.9 2.3 fusion.48
  440.2 4.0 gather_fusion
  444.5 2.8 gather_fusion.1
  447.7 2.3 fusion.48
  450.0 4.0 gather_fusion
  454.3 2.8 gather_fusion.1
  457.5 2.3 fusion.48
  459.8 4.0 gather_fusion
  464.1 2.8 gather_fusion.1
  467.3 2.3 fusion.48
  469.6 4.0 gather_fusion
  474.0 2.8 gather_fusion.1
  477.1 2.3 fusion.48
  479.4 4.0 gather_fusion
  483.8 2.8 gather_fusion.1
  486.9 2.3 fusion.48
  489.2 97.5 %all-gather.3.cloned.1.call-done = f32[128,128,128]{2,1,0:T(8,128)} async-done(((f32[16,128,128]{2,1,0:T(8,128)}), f32[128,128,128]{2,1,0:T(8,128)}) %all-gather.3.cloned.1.call-update) | async-done | bytes 8388624 | tf_op jit(solution)/shard_map/all_gather | solution.py:65
  586.7 4.2 reduce_sum.35
  590.9 1.6 divide_subtract_fusion
  (87 shorter events, 12.7 us)
Async XLA Ops:
  38.8 5.8 copy-start.1
  38.8 101.8 %all-to-all-start.2 = ((bf16[64,2,128,128]{3,2,1,0:T(8,128)(2,1)}), bf16[64,2,128,128]{3,2,1,0:T(8,128)(2,1)}, u32[]{:S(2)}, u32[]{:S(2)}) async-start(bf16[64,2,128,128]{3,2,1,0:T(8,128)(2,1)} %broadcast_select_fusion.1), calls=%async_computation.2 | async-start | bytes 8388608 | tf_op jit(solution)/shard_map/all_to_all | solution.py:36
  58.5 273.9 %copy-start = (bf16[40,128,128]{2,1,0:T(8,128)(2,1)S(1)}, bf16[40,128,128]{2,1,0:T(8,128)(2,1)}, u32[]{:S(2)}) copy-start(bf16[40,128,128]{2,1,0:T(8,128)(2,1)} %param.11) | copy-start | bytes 3932164
  140.6 191.8 %all-to-all-start.1 = ((bf16[64,2,256,128]{3,2,1,0:T(8,128)(2,1)}), bf16[64,2,256,128]{3,2,1,0:T(8,128)(2,1)}, u32[]{:S(2)}, u32[]{:S(2)}) async-start(bf16[64,2,256,128]{3,2,1,0:T(8,128)(2,1)} %broadcast_select_fusion), calls=%async_computation.1 | async-start | bytes 16777216 | tf_op jit(solution)/shard_map/all_to_all | solution.py:37
  146.6 440.1 %all-gather.3.cloned.1.call-start = ((), (), s32[]{:S(2)}) async-start(), calls=%async_computation.3 | async-start | bytes 9437184 | tf_op jit(solution)/shard_map/all_gather | solution.py:65
  586.7 4.2 copy-start.2
  586.7 4.2 copy-start.3
Sparse Core Ops, SparseCore 0:
  489.4 97.3 all-gather.2
